TPU v7x, 128 devices: a whole 4x4x4 slice. The times are simulated.
128 devices in a mesh: freq: 8 (over y, core), outp: 8 (over x, z_lo), inp: 2 (over z_hi).
Axes of the slice: x: 4, y: 4, z: 4 (z_hi: 2, z_lo: 2; z = z_hi * 2 + z_lo), core: 2. Of those that a mesh axis runs over, the one named last changes fastest.
Arguments:
- measured: float32 [2, 8, 2048, 2048], P(None, 'freq', 'outp', 'inp'), may hold values from -6 to 6
- left_factor: bfloat16 [2048, 4096], P('outp', 'freq'), may hold values from -0.75 to 0.75
- right_factor: bfloat16 [4096, 2048], P('freq', 'inp'), may hold values from -0.75 to 0.75
- pole_rates: float32 [512], replicated, may hold values from 0.5 to 8
- sample_freqs: float32 [8], P('freq'), may hold values from 0 to 8
Outputs:
- grad_left: float32 [2048, 4096], P('outp', ('freq', 'inp'))
- grad_right: float32 [4096, 2048], P(('freq', 'outp'), 'inp')
All inputs are finite; a program needn't handle non-finite values.
Results may differ from a plain program's by a relative error of at most 0.0003.
Values may be sent and summed in bfloat16 or wider, within the bound.
No kernel may reach another device: no remote copies, remote signals or barrier semaphores. Data moves between devices by JAX's collectives and lax.ppermute only.
A program may use at most 128 MiB of HBM per device.

v0:
```python
import math

import jax
import jax.numpy as jnp
from jax import lax
from jax.sharding import PartitionSpec as P

PORTS = 2048
RANK = 8
RANKS = 4096


def shards(measured, left_factor, right_factor, pole_rates, sample_freqs):
    highest = lax.Precision.HIGHEST
    left_whole = lax.all_gather(left_factor, "freq", axis=1, tiled=True)
    right_whole = lax.all_gather(right_factor, "freq", axis=0, tiled=True)
    local_samples = sample_freqs.shape[0]
    out_rows = left_whole.shape[0]
    in_cols = right_whole.shape[1]
    total_samples = local_samples * lax.axis_size("freq")
    grad_scale = float(RANKS) ** 0.25 / math.sqrt(float(total_samples * PORTS))
    left_wide = left_whole.astype(jnp.float32)
    right_wide = right_whole.astype(jnp.float32)
    omega = sample_freqs[0]
    denominator = pole_rates * pole_rates + omega * omega
    real_resp = jnp.repeat(pole_rates / denominator, RANK)
    imag_resp = jnp.repeat(-omega / denominator, RANK)
    scaled = jnp.concatenate([left_wide * real_resp[None, :], left_wide * imag_resp[None, :]], 0)
    fitted = jnp.dot(scaled, right_wide, precision=highest, preferred_element_type=jnp.float32)
    observed = measured[:, 0].reshape(2 * out_rows, in_cols)
    misfit = fitted - observed
    backward = lax.dot_general(
        misfit,
        right_wide,
        (((1,), (1,)), ((), ())),
        precision=highest,
        preferred_element_type=jnp.float32,
    )
    left_acc = backward[:out_rows] * real_resp[None, :] + backward[out_rows:] * imag_resp[None, :]
    left_term = left_acc * grad_scale
    grad_left = lax.psum_scatter(left_term, ("freq", "inp"), scatter_dimension=1, tiled=True)
    product = lax.dot_general(
        scaled,
        misfit,
        (((0,), (0,)), ((), ())),
        precision=highest,
        preferred_element_type=jnp.float32,
    )
    grad_right = lax.psum_scatter(
        product * grad_scale, ("freq", "outp"), scatter_dimension=0, tiled=True
    )
    return (grad_left, grad_right)


def solution(mesh):
    return jax.shard_map(
        shards,
        mesh=mesh,
        in_specs=(
            P(None, "freq", "outp", "inp"),
            P("outp", "freq"),
            P("freq", "inp"),
            P(),
            P("freq"),
        ),
        out_specs=(P("outp", ("freq", "inp")), P(("freq", "outp"), "inp")),
        check_vma=False,
    )
```

profile of v0, /device:TPU:0, one launch (start us, length us, event | category | flops | bytes accessed | tf_op | source)
XLA Modules:
  0.0 578.2 jit_solution(4097242679479421879)
XLA Ops:
  7.2 0.0 all-gather.3.cloned.1.call-start
  7.2 0.7 all-gather.3.cloned.1.call-update
  7.9 0.0 all-gather.5.cloned.1.call-start
  7.9 0.7 all-gather.5.cloned.1.call-update
  8.6 0.0 reduce-scatter.3.cloned.1.call-start
  9.3 0.7 fusion.5
  10.0 0.1 broadcast_in_dim.6
  10.2 0.2 mul.56
  10.3 0.1 broadcast_in_dim.7
  10.4 0.2 mul.59
  10.6 26.9 %all-gather.3.cloned.1.call-done = bf16[256,4096]{1,0:T(8,128)(2,1)} async-done(((bf16[256,512]{1,0:T(8,128)(2,1)}), bf16[256,4096]{1,0:T(8,128)(2,1)}) %all-gather.3.cloned.1.call-update) | async-done | bytes 2097168 | tf_op jit(solution)/shard_map/all_gather | solution.py:15
  37.5 5.9 %convert_multiply_fusion.1 = (f32[256,4096]{1,0:T(8,128)}, f32[256,4096]{1,0:T(8,128)}) fusion(bf16[256,4096]{1,0:T(8,128)(2,1)} %all-gather.3.cloned.1.call-done, f32[4096]{0:T(1024)S(1)} %mul.56, f32[4096]{0:T(1024)S(1)} %mul.59), kind=kLoop, calls=%fused_computation.5 | loop fusion | flops 3145728 | bytes 10518528 | tf_op jit(solution)/shard_map/mul | solution.py:28
  43.4 45.8 %all-gather.5.cloned.1.call-done = bf16[4096,1024]{1,0:T(8,128)(2,1)} async-done(((bf16[512,1024]{1,0:T(8,128)(2,1)}), bf16[4096,1024]{1,0:T(8,128)(2,1)}) %all-gather.5.cloned.1.call-update) | async-done | bytes 8388624 | tf_op jit(solution)/shard_map/all_gather | solution.py:16
  89.2 0.0 copy-start
  89.2 17.0 %bitcast_subtract_fusion = f32[512,1024]{1,0:T(8,128)S(1)} fusion(f32[2,1,256,1024]{3,2,1,0:T(8,128)} %param.5, bf16[4096,1024]{1,0:T(8,128)(2,1)} %all-gather.5.cloned.1.call-done, f32[256,4096]{1,0:T(8,128)} %get-tuple-element.3, f32[256,4096]{1,0:T(8,128)} %get-tuple-element.2), kind=kOutput, calls=%fused_computation.10 | convolution fusion | flops 25772425216 | bytes 20971520 | tf_op jit(solution)/shard_map/dot_general | solution.py:29
  106.2 0.0 copy-done
  106.3 13.6 %fusion.8 = f32[512,4096]{1,0:T(8,128)S(1)} fusion(f32[512,1024]{1,0:T(8,128)S(1)} %bitcast_subtract_fusion, bf16[4096,1024]{1,0:T(8,128)(2,1)S(1)} %copy-done), kind=kOutput, calls=%fused_computation.16 | convolution fusion | flops 25769803776 | bytes 18874368 | tf_op jit(solution)/shard_map/dot_general | solution.py:32
  119.8 2.8 fusion.3
  122.6 0.0 reduce-scatter.3.cloned.1.call-update
  122.6 0.2 reduce-scatter.5.cloned.1.call-start
  122.9 30.7 %broadcast_multiply_fusion = f32[4096,1024]{1,0:T(8,128)} fusion(f32[512,1024]{1,0:T(8,128)S(1)} %bitcast_subtract_fusion, f32[256,4096]{1,0:T(8,128)} %get-tuple-element.3, f32[256,4096]{1,0:T(8,128)} %get-tuple-element.2), kind=kOutput, calls=%fused_computation.1 | convolution fusion | flops 25776095232 | bytes 27262976 | tf_op jit(solution)/shard_map/dot_general | solution.py:42
  153.5 0.0 reduce-scatter.5.cloned.1.call-update
  153.6 50.1 %reduce-scatter.3.cloned.1.call-done = f32[256,256]{1,0:T(8,128)} async-done(((f32[256,4096]{1,0:T(8,128)}), f32[256,256]{1,0:T(8,128)}) %reduce-scatter.3.cloned.1.call-update) | async-done | bytes 262160 | tf_op jit(solution)/shard_map/reduce_scatter | solution.py:41
  203.7 368.0 %reduce-scatter.5.cloned.1.call-done = f32[64,1024]{1,0:T(8,128)} async-done(((f32[4096,1024]{1,0:T(8,128)}), f32[64,1024]{1,0:T(8,128)}) %reduce-scatter.5.cloned.1.call-update) | async-done | bytes 262160 | tf_op jit(solution)/shard_map/reduce_scatter | solution.py:49
Async XLA Ops:
  7.2 30.3 %all-gather.3.cloned.1.call-start = ((), (), s32[]{:S(2)}) async-start(), calls=%async_computation.2 | async-start | bytes 2359296 | tf_op jit(solution)/shard_map/all_gather | solution.py:15
  7.9 81.3 %all-gather.5.cloned.1.call-start = ((), (), s32[]{:S(2)}) async-start(), calls=%async_computation.3 | async-start | bytes 9437184 | tf_op jit(solution)/shard_map/all_gather | solution.py:16
  8.6 195.1 %reduce-scatter.3.cloned.1.call-start = ((), (), s32[]{:S(2)}) async-start(), calls=%async_computation.4 | async-start | bytes 4456448 | tf_op jit(solution)/shard_map/reduce_scatter | solution.py:41
  89.2 17.0 %copy-start = (bf16[4096,1024]{1,0:T(8,128)(2,1)S(1)}, bf16[4096,1024]{1,0:T(8,128)(2,1)}, u32[]{:S(2)}) copy-start(bf16[4096,1024]{1,0:T(8,128)(2,1)} %all-gather.5.cloned.1.call-done) | copy-start | bytes 25165828
  122.6 449.1 %reduce-scatter.5.cloned.1.call-start = ((), (), s32[]{:S(2)}) async-start(), calls=%async_computation.5 | async-start | bytes 17039360 | tf_op jit(solution)/shard_map/reduce_scatter | solution.py:49
Sparse Core Ops, SparseCore 0:
  9.7 27.7 all-gather.2
  39.2 49.9 all-gather.4
  122.8 80.9 reduce-scatter.2
  206.5 365.1 reduce-scatter.4
where the time goes:
time: 579 us; the launch traced here: 578 us
  waiting for transfers between devices  492 us (85%)
  matrix products  61.3 us (11%)
  between operations  14.5 us (3%)
  other arithmetic  9.32 us (2%)
    reduce_scatter x1, waiting for transfers between devices, shards(): lax.psum_scatter(product * grad_scale, ('freq', 'outp'), scatter_dimensio...  368 us
    reduce_scatter x1, waiting for transfers between devices, shards(): lax.psum_scatter(left_term, ('freq', 'inp'), scatter_dimension=1, tiled=T...  50.1 us
    all_gather x1, waiting for transfers between devices, shards(): right_whole = lax.all_gather(right_factor, 'freq', axis=0, tiled=True)  45.8 us
    dot_general x1, matrix products, shards(): lax.dot_general(scaled, misfit, (((0,), (0,)), ((), ())), precision=highe...  30.7 us
    all_gather x1, waiting for transfers between devices, shards(): left_whole = lax.all_gather(left_factor, 'freq', axis=1, tiled=True)  26.9 us
    dot_general x1, matrix products, shards(): jnp.dot(scaled, right_wide, precision=highest, preferred_element_type=jnp...  17 us
    dot_general x1, matrix products, shards(): lax.dot_general(misfit, right_wide, (((1,), (1,)), ((), ())), precision=h...  13.6 us
  transfers between devices with their start and end apart: 4, of which 4 were waited for; matrix products, arithmetic and copies ran while one was open for 7% of the time, Pallas kernels for 0%

commit v1 on v0

v1 whole, which is shorter than its diff:
```python
import math

import jax
import jax.numpy as jnp
from jax import lax
from jax.sharding import PartitionSpec as P

PORTS = 2048
RANK = 8
RANKS = 4096


def shards(measured, left_factor, right_factor, pole_rates, sample_freqs):
    highest = lax.Precision.HIGHEST
    n_freq = lax.axis_size("freq")
    n_outp = lax.axis_size("outp")
    observed = lax.all_to_all(measured, "freq", 3, 1, tiled=True)
    right_cols = lax.all_to_all(right_factor, "freq", 1, 0, tiled=True)
    left_whole = lax.all_gather(left_factor, "freq", axis=1, tiled=True)
    omegas = lax.all_gather(sample_freqs, "freq", axis=0, tiled=True)
    total_samples = omegas.shape[0]
    grad_scale = float(RANKS) ** 0.25 / math.sqrt(float(total_samples * PORTS))
    left_wide = left_whole.astype(jnp.float32)
    right_wide = right_cols.astype(jnp.float32)
    denominator = pole_rates[None, :] * pole_rates[None, :] + omegas[:, None] * omegas[:, None]
    real_resp = jnp.repeat(pole_rates[None, :] / denominator, RANK, axis=1)
    imag_resp = jnp.repeat(-omegas[:, None] / denominator, RANK, axis=1)
    resp = jnp.stack([real_resp, imag_resp], 0)
    scaled_right = resp[:, :, :, None] * right_wide[None, None]
    fitted = jnp.einsum("rk,pfkj->pfrj", left_wide, scaled_right, precision=highest,
                        preferred_element_type=jnp.float32)
    misfit = fitted - observed
    grad_left = jnp.einsum("pfrj,pfkj->rk", misfit, scaled_right, precision=highest,
                           preferred_element_type=jnp.float32)
    scaled_left = resp[:, :, None, :] * left_wide[None, None]
    grad_right = jnp.einsum("pfrk,pfrj->kj", scaled_left, misfit, precision=highest,
                            preferred_element_type=jnp.float32)
    grad_left = lax.psum_scatter(grad_left * grad_scale, ("freq", "inp"), scatter_dimension=1, tiled=True)
    k_rows, j_cols = grad_right.shape
    block = k_rows // (n_freq * n_outp)
    grad_right = (grad_right * grad_scale).reshape(n_freq, n_outp, block, j_cols)
    grad_right = grad_right.transpose(1, 0, 2, 3).reshape(n_outp * n_freq * block, j_cols)
    grad_right = lax.psum_scatter(grad_right, "outp", scatter_dimension=0, tiled=True)
    grad_right = grad_right.reshape(n_freq, block, j_cols)
    grad_right = lax.all_to_all(grad_right, "freq", 0, 2, tiled=True)
    grad_right = grad_right.reshape(block, n_freq * j_cols)
    return (grad_left, grad_right)


def solution(mesh):
    return jax.shard_map(
        shards,
        mesh=mesh,
        in_specs=(
            P(None, "freq", "outp", "inp"),
            P("outp", "freq"),
            P("freq", "inp"),
            P(),
            P("freq"),
        ),
        out_specs=(P("outp", ("freq", "inp")), P(("freq", "outp"), "inp")),
        check_vma=False,
    )
```

time: 579 us -> 366 us (0.63)
  waiting for transfers between devices: 492 us -> 91.3 us
  matrix products: 61.3 us -> 175 us
  blocking collectives: 0 us -> 40.8 us
  local copies, waits for them, and re-layouts: 0.55 us -> 28.7 us
  starting transfers between devices: 0.34 us -> 8.31 us
  other arithmetic: 9.32 us -> 1.7 us
    reduce_scatter x2, waiting for transfers between devices: 418 us -> 71.5 us  [the longest x1 71.5 us: shards(): lax.psum_scatter(grad_left * grad_scale, ('freq', 'inp'), scatter_dimensi...]
    dot_general x3, matrix products: 61.3 us -> 175 us  [the longest x1 72.3 us: shards(): jnp.einsum('pfrk,pfrj->kj', scaled_left, misfit, precision=highest, prefe...]
    all_gather x1 -> x0, waiting for transfers between devices: 45.8 us -> none  [shards(): right_whole = lax.all_gather(right_factor, 'freq', axis=0, tiled=True)]
    unnamed x0 -> x1, blocking collectives: none -> 29.9 us
    all_gather x1, waiting for transfers between devices: 26.9 us -> 0.01 us  [shards(): left_whole = lax.all_gather(left_factor, 'freq', axis=1, tiled=True)]
    all_to_all x0 -> x2, waiting for transfers between devices: none -> 19.1 us  [the longest x1 19.1 us: shards(): right_cols = lax.all_to_all(right_factor, 'freq', 1, 0, tiled=True)]
    all_to_all x0 -> x1, blocking collectives: none -> 10.8 us  [shards(): grad_right = lax.all_to_all(grad_right, 'freq', 0, 2, tiled=True)]
    mul x2 -> x1, other arithmetic: 8.63 us -> 0.01 us  [shards(): pole_rates[None, :] * pole_rates[None, :]]
  transfers between devices with their start and end apart: 4 -> 5, of which waited for: 4 -> 2; matrix products, arithmetic and copies ran while one was open for 7% -> 24% of each run, Pallas kernels for 0% -> 0%
where the time goes in v1:
time: 366 us; the launch traced here: 361 us
  matrix products  175 us (48%)
  waiting for transfers between devices  91.3 us (25%)
  blocking collectives  40.8 us (11%)
  local copies, waits for them, and re-layouts  28.7 us (8%)
  between operations  14.9 us (4%)
  starting transfers between devices  8.31 us (2%)
    dot_general x1, matrix products, shards(): jnp.einsum('pfrk,pfrj->kj', scaled_left, misfit, precision=highest, prefe...  72.3 us
    reduce_scatter x1, waiting for transfers between devices, shards(): lax.psum_scatter(grad_left * grad_scale, ('freq', 'inp'), scatter_dimensi...  71.5 us
    dot_general x1, matrix products, shards(): jnp.einsum('pfrj,pfkj->rk', misfit, scaled_right, precision=highest, pref...  64 us
    dot_general x1, matrix products, shards(): jnp.einsum('rk,pfkj->pfrj', left_wide, scaled_right, precision=highest, p...  38.7 us
    unnamed x1, blocking collectives  29.9 us
    all_to_all x1, waiting for transfers between devices, shards(): right_cols = lax.all_to_all(right_factor, 'freq', 1, 0, tiled=True)  19.1 us
    all_to_all x1, blocking collectives, shards(): grad_right = lax.all_to_all(grad_right, 'freq', 0, 2, tiled=True)  10.8 us
    unnamed x18, local copies, waits for them, and re-layouts  8.43 us
  transfers between devices with their start and end apart: 5, of which 2 were waited for; matrix products, arithmetic and copies ran while one was open for 24% of the time, Pallas kernels for 0%

profile of v1, /device:TPU:0, one launch (start us, length us, event | category | flops | bytes accessed | tf_op | source)
XLA Modules:
  0.0 360.6 jit_solution(8278034630657662266)
XLA Ops:
  7.2 0.0 all-gather.2.cloned.1.call-start
  7.2 0.7 all-gather.2.cloned.1.call-update
  7.9 0.0 copy-start.2
  7.9 2.4 copy.44
  10.4 4.6 %all-to-all-start = ((bf16[512,8,128]{0,2,1:T(8,128)(2,1)}), bf16[512,8,128]{0,2,1:T(8,128)(2,1)S(1)}, u32[]{:S(2)}, u32[]{:S(2)}) async-start(bf16[512,8,128]{0,2,1:T(8,128)(2,1)} %bitcast.1), calls=%async_computation | async-start | bytes 2097152 | tf_op jit(solution)/shard_map/all_to_all | solution.py:18
  14.9 0.0 copy-done.2
  14.9 2.4 copy.47
  17.3 0.0 copy-start.5
  17.3 0.0 copy-start.4
  17.3 19.1 %all-to-all-done = bf16[512,8,128]{0,2,1:T(8,128)(2,1)S(1)} async-done(((bf16[512,8,128]{0,2,1:T(8,128)(2,1)}), bf16[512,8,128]{0,2,1:T(8,128)(2,1)S(1)}, u32[]{:S(2)}, u32[]{:S(2)}) %all-to-all-start) | async-done | bytes 1048608 | tf_op jit(solution)/shard_map/all_to_all | solution.py:18
  36.4 3.6 all-to-all-start.1
  40.0 0.0 reduce-scatter.5.cloned.1.call-start
  40.7 0.0 copy-done.5
  40.7 0.6 dynamic-slice
  41.3 0.8 dynamic-update-slice
  42.1 29.9 %all-reduce = f32[8]{0:T(128)S(1)} all-reduce(f32[8]{0:T(128)S(1)} %dynamic-update-slice), channel_id=1, replica_groups=mesh['freq'=8,'outp'=8,'inp'=2] {'freq'}, use_global_device_ids=true, to_apply=%add | all-reduce | flops 8 | bytes 64
  72.0 0.0 copy-done.4
  72.0 0.1 add_divide_fusion.1
  72.1 1.9 broadcast_in_dim.4
  74.0 2.8 stack_reshape.6
  76.8 1.9 broadcast_in_dim.5
  78.7 2.8 stack_reshape.7
  81.5 0.2 copy.43
  81.7 1.6 convert_bitcast_fusion
  83.3 2.9 copy.45
  86.3 0.0 all-to-all-done.1
  86.3 1.5 copy.48
  87.8 0.0 all-gather.2.cloned.1.call-done
  87.8 0.0 copy-start.1
  87.8 4.5 %copy.51 = f32[256,4096]{0,1:T(8,128)} copy(bf16[256,4096]{1,0:T(8,128)(2,1)} %all-gather.2.cloned.1.call-done) | data formatting | bytes 6291456 | tf_op jit(solution)/shard_map/convert_element_type | solution.py:23
  92.3 0.0 copy-done.1
  92.3 0.0 copy-start
  92.3 38.7 %bitcast_subtract_fusion = f32[2,8,256,128]{2,3,1,0:T(8,128)} fusion(f32[2,8,256,128]{2,3,1,0:T(8,128)} %bitcast.50, bf16[256,4096]{1,0:T(8,128)(2,1)S(1)} %copy-done.1, f32[4096,128]{1,0:T(8,128)} %bitcast.48, f32[2,8,4096]{2,0,1:T(2,128)S(1)} %copy.43), kind=kOutput, calls=%fused_computation.13 | convolution fusion | flops 25778716672 | bytes 8650752 | tf_op jit(solution)/shard_map/rk,pfkj->pfrj/dot_general | solution.py:30
  130.9 0.0 copy-done
  130.9 72.3 %fusion.12 = f32[4096,128]{1,0:T(8,128)S(1)} fusion(f32[256,4096]{0,1:T(8,128)S(1)} %copy-done, f32[2,8,4096]{2,0,1:T(2,128)S(1)} %copy.43, f32[2,8,256,128]{2,3,1,0:T(8,128)} %bitcast_subtract_fusion), kind=kOutput, calls=%fused_computation.11 | convolution fusion | flops 25787105280 | bytes 8650752 | tf_op jit(solution)/shard_map/pfrk,pfrj->kj/dot_general | solution.py:36
  203.2 1.6 copy.53
  204.8 0.0 copy-start.3
  204.8 0.0 reduce-scatter.5.cloned.1.call-update
  204.8 0.0 reduce-scatter.3.cloned.1.call-start
  204.9 1.5 copy-done.3
  206.4 64.0 %fusion.8 = f32[256,4096]{1,0:T(8,128)} fusion(f32[4096,128]{1,0:T(8,128)S(1)} %bitcast.49, f32[2,8,4096]{2,0,1:T(2,128)S(1)} %copy.43, f32[2,8,256,128]{2,3,1,0:T(8,128)} %bitcast_subtract_fusion), kind=kOutput, calls=%fused_computation.9 | convolution fusion | flops 25779240960 | bytes 8650752 | tf_op jit(solution)/shard_map/pfrj,pfkj->rk/dot_general | solution.py:33
  270.5 0.0 reduce-scatter.3.cloned.1.call-update
  270.5 0.0 reduce-scatter.5.cloned.1.call-done
  270.5 10.8 %all_to_all.46 = f32[8,64,128]{2,1,0:T(8,128)S(1)} all-to-all(f32[8,64,128]{2,1,0:T(8,128)} %bitcast.54), channel_id=1, replica_groups=mesh['freq'=8,'outp'=8,'inp'=2] {'freq'}, dimensions={0} | all-to-all | bytes 524288 | tf_op jit(solution)/shard_map/all_to_all | solution.py:45
  281.3 0.2 copy.54
  281.5 0.8 copy.77
  282.2 71.5 %reduce-scatter.3.cloned.1.call-done = f32[256,256]{1,0:T(8,128)} async-done(((f32[256,4096]{1,0:T(8,128)}), f32[256,256]{1,0:T(8,128)}) %reduce-scatter.3.cloned.1.call-update) | async-done | bytes 262160 | tf_op jit(solution)/shard_map/reduce_scatter | solution.py:38
  (4 shorter events, 0.0 us)
Async XLA Ops:
  7.2 80.6 %all-gather.2.cloned.1.call-start = ((), (), s32[]{:S(2)}) async-start(), calls=%async_computation.5 | async-start | bytes 2359296 | tf_op jit(solution)/shard_map/all_gather | solution.py:19
  7.9 7.0 %copy-start.2 = (f32[2,1,256,1024]{3,2,1,0:T(8,128)S(1)}, f32[2,1,256,1024]{3,2,1,0:T(8,128)}, u32[]{:S(2)}) copy-start(f32[2,1,256,1024]{3,2,1,0:T(8,128)} %param.5) | copy-start | bytes 6291460
  10.4 26.1 %all-to-all-start = ((bf16[512,8,128]{0,2,1:T(8,128)(2,1)}), bf16[512,8,128]{0,2,1:T(8,128)(2,1)S(1)}, u32[]{:S(2)}, u32[]{:S(2)}) async-start(bf16[512,8,128]{0,2,1:T(8,128)(2,1)} %bitcast.1), calls=%async_computation | async-start | bytes 2097152 | tf_op jit(solution)/shard_map/all_to_all | solution.py:18
  17.3 23.4 %copy-start.5 = (u32[128]{0:T(128)S(1)}, u32[128]{0:T(128)}, u32[]{:S(2)}) copy-start(u32[128]{0:T(128)} %constant.7) | copy-start | bytes 1540
  17.3 54.7 %copy-start.4 = (f32[512]{0:T(512)S(1)}, f32[512]{0:T(512)}, u32[]{:S(2)}) copy-start(f32[512]{0:T(512)} %param.8) | copy-start | bytes 6148
  36.4 49.8 %all-to-all-start.1 = ((f32[2,1,256,1024]{2,0,1,3:T(2,128)}), f32[2,1,256,1024]{2,0,1,3:T(2,128)S(1)}, u32[]{:S(2)}, u32[]{:S(2)}) async-start(f32[2,1,256,1024]{2,0,1,3:T(2,128)} %copy.47), calls=%async_computation.1 | async-start | bytes 4194304 | tf_op jit(solution)/shard_map/all_to_all | solution.py:17
  40.0 230.5 %reduce-scatter.5.cloned.1.call-start = ((), (), s32[]{:S(2)}) async-start(), calls=%async_computation.7 | async-start | bytes 2359296 | tf_op jit(solution)/shard_map/reduce_scatter | solution.py:43
  87.8 4.5 %copy-start.1 = (bf16[256,4096]{1,0:T(8,128)(2,1)S(1)}, bf16[256,4096]{1,0:T(8,128)(2,1)}, u32[]{:S(2)}) copy-start(bf16[256,4096]{1,0:T(8,128)(2,1)} %all-gather.2.cloned.1.call-done) | copy-start | bytes 6291460
  92.3 38.7 %copy-start = (f32[256,4096]{0,1:T(8,128)S(1)}, f32[256,4096]{0,1:T(8,128)}, u32[]{:S(2)}) copy-start(f32[256,4096]{0,1:T(8,128)} %copy.51) | copy-start | bytes 12582916
  204.8 1.6 copy-start.3
  204.8 148.9 %reduce-scatter.3.cloned.1.call-start = ((), (), s32[]{:S(2)}) async-start(), calls=%async_computation.6 | async-start | bytes 4456448 | tf_op jit(solution)/shard_map/reduce_scatter | solution.py:38
Sparse Core Ops, SparseCore 0:
  9.7 31.1 all-gather.1
  205.0 53.9 reduce-scatter.4
  270.6 83.0 reduce-scatter.2

commit v2 on v1

--- a/solution.py
+++ b/solution.py
@@ -11,13 +11,17 @@
 
 
 def shards(measured, left_factor, right_factor, pole_rates, sample_freqs):
-    highest = lax.Precision.HIGHEST
+    highest = lax.Precision.HIGH
     n_freq = lax.axis_size("freq")
     n_outp = lax.axis_size("outp")
-    observed = lax.all_to_all(measured, "freq", 3, 1, tiled=True)
+    two, _, out_rows, in_cols = measured.shape
+    tagged = jnp.concatenate(
+        [measured, jnp.broadcast_to(sample_freqs[0], (two, 1, 8, in_cols))], axis=2)
+    tagged = lax.all_to_all(tagged, "freq", 3, 1, tiled=True)
+    observed = tagged[:, :, :out_rows, :]
+    omegas = tagged[0, :, out_rows, 0]
     right_cols = lax.all_to_all(right_factor, "freq", 1, 0, tiled=True)
     left_whole = lax.all_gather(left_factor, "freq", axis=1, tiled=True)
-    omegas = lax.all_gather(sample_freqs, "freq", axis=0, tiled=True)
     total_samples = omegas.shape[0]
     grad_scale = float(RANKS) ** 0.25 / math.sqrt(float(total_samples * PORTS))
     left_wide = left_whole.astype(jnp.float32)

time: 366 us -> 305 us (0.83)
  matrix products: 175 us -> 101 us
  waiting for transfers between devices: 91.3 us -> 135 us
  blocking collectives: 40.8 us -> 12.6 us
    dot_general x1, matrix products: 72.3 us -> 32.1 us  [shards(): jnp.einsum('pfrk,pfrj->kj', scaled_left, misfit, precision=highest, prefe...]
    all_to_all x1, waiting for transfers between devices: 0.01 us -> 32.5 us  [shards(): tagged = lax.all_to_all(tagged, 'freq', 3, 1, tiled=True)]
    unnamed x1 -> x0, blocking collectives: 29.9 us -> none
    dot_general x1, matrix products: 64 us -> 38.1 us  [shards(): jnp.einsum('pfrj,pfkj->rk', misfit, scaled_right, precision=highest, pref...]
    reduce_scatter x1, waiting for transfers between devices: 0.02 us -> 13.6 us  [shards(): lax.psum_scatter(grad_right, 'outp', scatter_dimension=0, tiled=True)]
    dot_general x1, matrix products: 38.7 us -> 30.2 us  [shards(): jnp.einsum('rk,pfkj->pfrj', left_wide, scaled_right, precision=highest, p...]
    all_to_all x1, waiting for transfers between devices: 19.1 us -> 15.2 us  [shards(): right_cols = lax.all_to_all(right_factor, 'freq', 1, 0, tiled=True)]
    unnamed x18 -> x15, local copies, waits for them, and re-layouts: 8.43 us -> 9.84 us
  transfers between devices with their start and end apart: 5 -> 5, of which waited for: 2 -> 4; matrix products, arithmetic and copies ran while one was open for 24% -> 19% of each run, Pallas kernels for 0% -> 0%
where the time goes in v2:
time: 305 us; the launch traced here: 300 us
  waiting for transfers between devices  135 us (44%)
  matrix products  101 us (33%)
  local copies, waits for them, and re-layouts  25.5 us (8%)
  between operations  14.7 us (5%)
  blocking collectives  12.6 us (4%)
  starting transfers between devices  8.35 us (3%)
  other arithmetic  3.1 us (1%)
    reduce_scatter x1, waiting for transfers between devices, shards(): lax.psum_scatter(grad_left * grad_scale, ('freq', 'inp'), scatter_dimensi...  72.8 us
    dot_general x1, matrix products, shards(): jnp.einsum('pfrj,pfkj->rk', misfit, scaled_right, precision=highest, pref...  38.1 us
    all_to_all x1, waiting for transfers between devices, shards(): tagged = lax.all_to_all(tagged, 'freq', 3, 1, tiled=True)  32.5 us
    dot_general x1, matrix products, shards(): jnp.einsum('pfrk,pfrj->kj', scaled_left, misfit, precision=highest, prefe...  32.1 us
    dot_general x1, matrix products, shards(): jnp.einsum('rk,pfkj->pfrj', left_wide, scaled_right, precision=highest, p...  30.2 us
    all_to_all x1, waiting for transfers between devices, shards(): right_cols = lax.all_to_all(right_factor, 'freq', 1, 0, tiled=True)  15.2 us
    reduce_scatter x1, waiting for transfers between devices, shards(): lax.psum_scatter(grad_right, 'outp', scatter_dimension=0, tiled=True)  13.6 us
    all_to_all x1, blocking collectives, shards(): grad_right = lax.all_to_all(grad_right, 'freq', 0, 2, tiled=True)  12.6 us
  transfers between devices with their start and end apart: 5, of which 4 were waited for; matrix products, arithmetic and copies ran while one was open for 19% of the time, Pallas kernels for 0%

profile of v2, /device:TPU:0, one launch (start us, length us, event | category | flops | bytes accessed | tf_op | source)
XLA Modules:
  0.0 299.6 jit_solution(6700158223750506833)
XLA Ops:
  7.2 0.0 all-gather.2.cloned.1.call-start
  7.2 0.7 all-gather.2.cloned.1.call-update
  7.9 2.3 copy.46
  10.2 4.6 %all-to-all-start.1 = ((bf16[512,8,128]{0,2,1:T(8,128)(2,1)}), bf16[512,8,128]{0,2,1:T(8,128)(2,1)S(1)}, u32[]{:S(2)}, u32[]{:S(2)}) async-start(bf16[512,8,128]{0,2,1:T(8,128)(2,1)} %bitcast.4), calls=%async_computation.1 | async-start | bytes 2097152 | tf_op jit(solution)/shard_map/all_to_all | solution.py:23
  15.4 2.9 copy.43
  18.3 2.6 concatenate.3
  20.9 0.0 copy-start.5
  20.9 15.2 %all-to-all-done.1 = bf16[512,8,128]{0,2,1:T(8,128)(2,1)S(1)} async-done(((bf16[512,8,128]{0,2,1:T(8,128)(2,1)}), bf16[512,8,128]{0,2,1:T(8,128)(2,1)S(1)}, u32[]{:S(2)}, u32[]{:S(2)}) %all-to-all-start.1) | async-done | bytes 1048608 | tf_op jit(solution)/shard_map/all_to_all | solution.py:23
  36.1 0.0 copy-start
  36.1 1.0 copy-done
  37.1 3.6 %all-to-all-start = ((f32[2,1,264,1024]{2,0,1,3:T(2,128)}), f32[2,1,264,1024]{2,0,1,3:T(2,128)S(1)}, u32[]{:S(2)}, u32[]{:S(2)}) async-start(f32[2,1,264,1024]{2,0,1,3:T(2,128)} %concatenate.3), calls=%async_computation | async-start | bytes 6291456 | tf_op jit(solution)/shard_map/all_to_all | solution.py:20
  40.7 0.0 reduce-scatter.5.cloned.1.call-start
  40.8 0.0 copy-done.5
  40.8 2.9 convert_bitcast_fusion
  43.6 2.9 copy.47
  46.5 32.5 %all-to-all-done = f32[2,1,264,1024]{2,0,1,3:T(2,128)S(1)} async-done(((f32[2,1,264,1024]{2,0,1,3:T(2,128)}), f32[2,1,264,1024]{2,0,1,3:T(2,128)S(1)}, u32[]{:S(2)}, u32[]{:S(2)}) %all-to-all-start) | async-done | bytes 2162720 | tf_op jit(solution)/shard_map/all_to_all | solution.py:20
  79.0 0.2 copy.44
  79.3 0.0 copy-start.2
  79.3 0.1 multiply_reduce_fusion
  79.4 0.1 add_divide_fusion.1
  79.5 1.4 copy-done.2
  80.9 0.6 broadcast_in_dim.4
  81.5 1.2 stack_reshape.6
  82.7 0.6 broadcast_in_dim.5
  83.3 1.2 stack_reshape.7
  84.5 0.2 copy.45
  84.8 0.0 all-gather.2.cloned.1.call-done
  84.8 0.0 copy-start.3
  84.8 4.5 %copy.51 = f32[256,4096]{0,1:T(8,128)} copy(bf16[256,4096]{1,0:T(8,128)(2,1)} %all-gather.2.cloned.1.call-done) | data formatting | bytes 6291456 | tf_op jit(solution)/shard_map/convert_element_type | solution.py:27
  89.3 0.0 copy-done.3
  89.3 0.0 copy-start.1
  89.3 30.2 %slice_subtract_fusion = f32[2,8,256,128]{2,3,1,0:T(8,128)} fusion(f32[2,8,264,128]{2,3,1,0:T(8,128)} %bitcast.47, bf16[256,4096]{1,0:T(8,128)(2,1)S(1)} %copy-done.3, f32[4096,128]{1,0:T(8,128)} %bitcast.48, f32[2,8,4096]{2,0,1:T(2,128)S(1)} %copy.45), kind=kOutput, calls=%fused_computation.12 | convolution fusion | flops 12893814784 | bytes 8650752 | tf_op jit(solution)/shard_map/rk,pfkj->pfrj/dot_general | solution.py:34
  119.5 0.0 copy-done.1
  119.5 32.1 %fusion.12 = f32[4096,128]{1,0:T(8,128)S(1)} fusion(f32[256,4096]{0,1:T(8,128)S(1)} %copy-done.1, f32[2,8,4096]{2,0,1:T(2,128)S(1)} %copy.45, f32[2,8,256,128]{2,3,1,0:T(8,128)} %slice_subtract_fusion), kind=kOutput, calls=%fused_computation.11 | convolution fusion | flops 12902203392 | bytes 8650752 | tf_op jit(solution)/shard_map/pfrk,pfrj->kj/dot_general | solution.py:40
  151.7 1.6 copy.53
  153.2 0.0 copy-start.4
  153.2 0.0 reduce-scatter.5.cloned.1.call-update
  153.3 0.0 reduce-scatter.3.cloned.1.call-start
  153.3 1.5 copy-done.4
  154.8 38.1 %fusion.8 = f32[256,4096]{1,0:T(8,128)} fusion(f32[4096,128]{1,0:T(8,128)S(1)} %bitcast.49, f32[2,8,4096]{2,0,1:T(2,128)S(1)} %copy.45, f32[2,8,256,128]{2,3,1,0:T(8,128)} %slice_subtract_fusion), kind=kOutput, calls=%fused_computation.9 | convolution fusion | flops 12894339072 | bytes 8650752 | tf_op jit(solution)/shard_map/pfrj,pfkj->rk/dot_general | solution.py:37
  192.9 0.0 reduce-scatter.3.cloned.1.call-update
  193.0 13.6 %reduce-scatter.5.cloned.1.call-done = f32[512,128]{1,0:T(8,128)} async-done(((f32[4096,128]{1,0:T(8,128)}), f32[512,128]{1,0:T(8,128)}) %reduce-scatter.5.cloned.1.call-update) | async-done | bytes 262160 | tf_op jit(solution)/shard_map/reduce_scatter | solution.py:47
  206.6 12.6 %all_to_all.46 = f32[8,64,128]{2,1,0:T(8,128)S(1)} all-to-all(f32[8,64,128]{2,1,0:T(8,128)} %bitcast.53), channel_id=1, replica_groups=mesh['freq'=8,'outp'=8,'inp'=2] {'freq'}, dimensions={0} | all-to-all | bytes 524288 | tf_op jit(solution)/shard_map/all_to_all | solution.py:49
  219.1 0.2 copy.54
  219.3 0.8 copy.74
  220.1 72.8 %reduce-scatter.3.cloned.1.call-done = f32[256,256]{1,0:T(8,128)} async-done(((f32[256,4096]{1,0:T(8,128)}), f32[256,256]{1,0:T(8,128)}) %reduce-scatter.3.cloned.1.call-update) | async-done | bytes 262160 | tf_op jit(solution)/shard_map/reduce_scatter | solution.py:42
  (2 shorter events, 0.0 us)
Async XLA Ops:
  7.2 77.6 %all-gather.2.cloned.1.call-start = ((), (), s32[]{:S(2)}) async-start(), calls=%async_computation.5 | async-start | bytes 2359296 | tf_op jit(solution)/shard_map/all_gather | solution.py:24
  10.2 25.9 %all-to-all-start.1 = ((bf16[512,8,128]{0,2,1:T(8,128)(2,1)}), bf16[512,8,128]{0,2,1:T(8,128)(2,1)S(1)}, u32[]{:S(2)}, u32[]{:S(2)}) async-start(bf16[512,8,128]{0,2,1:T(8,128)(2,1)} %bitcast.4), calls=%async_computation.1 | async-start | bytes 2097152 | tf_op jit(solution)/shard_map/all_to_all | solution.py:23
  20.9 19.9 %copy-start.5 = (f32[512]{0:T(512)S(1)}, f32[512]{0:T(512)}, u32[]{:S(2)}) copy-start(f32[512]{0:T(512)} %param.8) | copy-start | bytes 6148
  36.1 1.0 copy-start
  37.1 42.0 %all-to-all-start = ((f32[2,1,264,1024]{2,0,1,3:T(2,128)}), f32[2,1,264,1024]{2,0,1,3:T(2,128)S(1)}, u32[]{:S(2)}, u32[]{:S(2)}) async-start(f32[2,1,264,1024]{2,0,1,3:T(2,128)} %concatenate.3), calls=%async_computation | async-start | bytes 6291456 | tf_op jit(solution)/shard_map/all_to_all | solution.py:20
  40.7 165.8 %reduce-scatter.5.cloned.1.call-start = ((), (), s32[]{:S(2)}) async-start(), calls=%async_computation.7 | async-start | bytes 2359296 | tf_op jit(solution)/shard_map/reduce_scatter | solution.py:47
  79.3 1.7 copy-start.2
  84.8 4.5 %copy-start.3 = (bf16[256,4096]{1,0:T(8,128)(2,1)S(1)}, bf16[256,4096]{1,0:T(8,128)(2,1)}, u32[]{:S(2)}) copy-start(bf16[256,4096]{1,0:T(8,128)(2,1)} %all-gather.2.cloned.1.call-done) | copy-start | bytes 6291460
  89.3 30.3 %copy-start.1 = (f32[256,4096]{0,1:T(8,128)S(1)}, f32[256,4096]{0,1:T(8,128)}, u32[]{:S(2)}) copy-start(f32[256,4096]{0,1:T(8,128)} %copy.51) | copy-start | bytes 12582916
  153.2 1.6 copy-start.4
  153.3 139.6 %reduce-scatter.3.cloned.1.call-start = ((), (), s32[]{:S(2)}) async-start(), calls=%async_computation.6 | async-start | bytes 4456448 | tf_op jit(solution)/shard_map/reduce_scatter | solution.py:42
Sparse Core Ops, SparseCore 0:
  9.7 30.9 all-gather.1
  153.4 53.1 reduce-scatter.4
  211.2 81.6 reduce-scatter.2

commit v3 on v1

v3 whole, which is shorter than its diff:
```python
import math

import jax
import jax.numpy as jnp
from jax import lax
from jax.sharding import PartitionSpec as P

PORTS = 2048
RANK = 8
RANKS = 4096


def shards(measured, left_factor, right_factor, pole_rates, sample_freqs):
    precision = lax.Precision.HIGH
    n_freq = lax.axis_size("freq")
    n_outp = lax.axis_size("outp")
    two, _, out_rows, in_cols = measured.shape
    half = out_rows // 2
    first = jnp.concatenate(
        [measured[:, :, :half], jnp.broadcast_to(sample_freqs[0], (two, 1, 8, in_cols))], axis=2)
    first = lax.all_to_all(first, "freq", 3, 1, tiled=True)
    omegas = first[0, :, half, 0]
    observed = (first[:, :, :half], lax.all_to_all(measured[:, :, half:], "freq", 3, 1, tiled=True))
    right_cols = lax.all_to_all(right_factor, "freq", 1, 0, tiled=True)
    left_whole = lax.all_gather(left_factor, "freq", axis=1, tiled=True)
    total_samples = omegas.shape[0]
    grad_scale = float(RANKS) ** 0.25 / math.sqrt(float(total_samples * PORTS))
    right_wide = right_cols.astype(jnp.float32)
    denominator = pole_rates[None, :] * pole_rates[None, :] + omegas[:, None] * omegas[:, None]
    real_resp = jnp.repeat(pole_rates[None, :] / denominator, RANK, axis=1)
    imag_resp = jnp.repeat(-omegas[:, None] / denominator, RANK, axis=1)
    resp = jnp.stack([real_resp, imag_resp], 0)
    scaled_right = resp[:, :, :, None] * right_wide[None, None]
    grad_left = []
    grad_right = None
    for h in range(2):
        left_wide = left_whole[h * half:(h + 1) * half].astype(jnp.float32)
        fitted = jnp.einsum("rk,pfkj->pfrj", left_wide, scaled_right, precision=precision,
                            preferred_element_type=jnp.float32)
        misfit = fitted - observed[h]
        part = jnp.einsum("pfrj,pfkj->rk", misfit, scaled_right, precision=precision,
                          preferred_element_type=jnp.float32)
        grad_left.append(lax.psum_scatter(part * grad_scale, ("freq", "inp"),
                                          scatter_dimension=1, tiled=True))
        scaled_left = resp[:, :, None, :] * left_wide[None, None]
        term = jnp.einsum("pfrk,pfrj->kj", scaled_left, misfit, precision=precision,
                          preferred_element_type=jnp.float32)
        grad_right = term if grad_right is None else grad_right + term
    grad_left = jnp.concatenate(grad_left, 0)
    k_rows, j_cols = grad_right.shape
    block = k_rows // (n_freq * n_outp)
    grad_right = (grad_right * grad_scale).reshape(n_freq, n_outp, block, j_cols)
    grad_right = lax.all_to_all(grad_right, "outp", 1, 1, tiled=True)
    grad_right = jnp.sum(grad_right, axis=1)
    grad_right = lax.all_to_all(grad_right, "freq", 0, 2, tiled=True)
    grad_right = grad_right.reshape(block, n_freq * j_cols)
    return (grad_left, grad_right)


def solution(mesh):
    return jax.shard_map(
        shards,
        mesh=mesh,
        in_specs=(
            P(None, "freq", "outp", "inp"),
            P("outp", "freq"),
            P("freq", "inp"),
            P(),
            P("freq"),
        ),
        out_specs=(P("outp", ("freq", "inp")), P(("freq", "outp"), "inp")),
        check_vma=False,
    )
```

time: 366 us -> 345 us (0.943)
  waiting for transfers between devices: 91.3 us -> 71.4 us
  matrix products: 175 us -> 164 us
  other arithmetic: 1.7 us -> 8.45 us
  local copies, waits for them, and re-layouts: 28.7 us -> 23 us
  blocking collectives: 40.8 us -> 45.8 us
  starting transfers between devices: 8.31 us -> 12.7 us
    reduce_scatter x2, waiting for transfers between devices: 71.5 us -> 18.7 us  [shards(): lax.psum_scatter(part * grad_scale, ('freq', 'inp'), scatter_dimension=1,...]
    all_to_all x0 -> x1, blocking collectives: none -> 34.3 us  [shards(): grad_right = lax.all_to_all(grad_right, 'outp', 1, 1, tiled=True)]
    all_to_all x1 -> x2, waiting for transfers between devices: 0.01 us -> 31.8 us  [the longest x1 20.2 us: shards(): first = lax.all_to_all(first, 'freq', 3, 1, tiled=True)]
    unnamed x1 -> x0, blocking collectives: 29.9 us -> none
    dot_general x3 -> x6, matrix products: 175 us -> 164 us  [the longest x2 71.6 us: shards(): jnp.einsum('rk,pfkj->pfrj', left_wide, scaled_right, precision=precision,...]
    all_to_all x1 -> x2, starting transfers between devices: 3.6 us -> 7.85 us  [the longest x1 4.25 us: shards(): lax.all_to_all(measured[:, :, half:], 'freq', 3, 1, tiled=True)]
    unnamed x18 -> x19, local copies, waits for them, and re-layouts: 8.43 us -> 6.53 us
  transfers between devices with their start and end apart: 5 -> 6, of which waited for: 2 -> 4; matrix products, arithmetic and copies ran while one was open for 24% -> 36% of each run, Pallas kernels for 0% -> 0%
where the time goes in v3:
time: 345 us; the launch traced here: 340 us
  matrix products  164 us (48%)
  waiting for transfers between devices  71.4 us (21%)
  blocking collectives  45.8 us (13%)
  local copies, waits for them, and re-layouts  23 us (7%)
  between operations  14.8 us (4%)
  starting transfers between devices  12.7 us (4%)
  other arithmetic  8.45 us (2%)
    dot_general x2, matrix products, shards(): jnp.einsum('rk,pfkj->pfrj', left_wide, scaled_right, precision=precision,...  71.6 us
    dot_general x2, matrix products, shards(): jnp.einsum('pfrj,pfkj->rk', misfit, scaled_right, precision=precision, pr...  51.8 us
    dot_general x2, matrix products, shards(): jnp.einsum('pfrk,pfrj->kj', scaled_left, misfit, precision=precision, pre...  40.5 us
    all_to_all x1, blocking collectives, shards(): grad_right = lax.all_to_all(grad_right, 'outp', 1, 1, tiled=True)  34.3 us
    all_to_all x1, waiting for transfers between devices, shards(): first = lax.all_to_all(first, 'freq', 3, 1, tiled=True)  20.2 us
    all_to_all x1, waiting for transfers between devices, shards(): right_cols = lax.all_to_all(right_factor, 'freq', 1, 0, tiled=True)  20.1 us
    reduce_scatter x2, waiting for transfers between devices, shards(): lax.psum_scatter(part * grad_scale, ('freq', 'inp'), scatter_dimension=1,...  18.7 us
    all_to_all x1, waiting for transfers between devices, shards(): lax.all_to_all(measured[:, :, half:], 'freq', 3, 1, tiled=True)  11.6 us
  transfers between devices with their start and end apart: 6, of which 4 were waited for; matrix products, arithmetic and copies ran while one was open for 36% of the time, Pallas kernels for 0%

profile of v3, /device:TPU:0, one launch (start us, length us, event | category | flops | bytes accessed | tf_op | source)
XLA Modules:
  0.0 340.0 jit_solution(12544909922784567064)
XLA Ops:
  7.2 0.0 all-gather.2.cloned.1.call-start
  7.2 0.7 all-gather.2.cloned.1.call-update
  7.9 2.3 copy.108
  10.2 0.0 slice-start
  10.2 4.7 %all-to-all-start.1 = ((bf16[512,8,128]{0,2,1:T(8,128)(2,1)}), bf16[512,8,128]{0,2,1:T(8,128)(2,1)S(1)}, u32[]{:S(2)}, u32[]{:S(2)}) async-start(bf16[512,8,128]{0,2,1:T(8,128)(2,1)} %bitcast.4), calls=%async_computation.1 | async-start | bytes 2097152 | tf_op jit(solution)/shard_map/all_to_all | solution.py:24
  14.9 0.0 slice-done
  14.9 0.0 copy-start.5
  14.9 1.3 copy.143
  16.2 20.1 %all-to-all-done.1 = bf16[512,8,128]{0,2,1:T(8,128)(2,1)S(1)} async-done(((bf16[512,8,128]{0,2,1:T(8,128)(2,1)}), bf16[512,8,128]{0,2,1:T(8,128)(2,1)S(1)}, u32[]{:S(2)}, u32[]{:S(2)}) %all-to-all-start.1) | async-done | bytes 1048608 | tf_op jit(solution)/shard_map/all_to_all | solution.py:24
  36.4 4.2 %all-to-all-start.2 = ((f32[2,1,128,1024]{2,0,1,3:T(2,128)}), f32[2,1,128,1024]{2,0,1,3:T(2,128)}, u32[]{:S(2)}, u32[]{:S(2)}) async-start(f32[2,1,128,1024]{2,0,1,3:T(2,128)} %copy.143), calls=%async_computation.3 | async-start | bytes 2097152 | tf_op jit(solution)/shard_map/all_to_all | solution.py:23
  41.3 0.0 copy-done.5
  41.3 1.4 slice_select_fusion
  42.7 2.3 copy.105
  45.0 0.0 copy-start.4
  45.0 11.6 %all-to-all-done.2 = f32[2,1,128,1024]{2,0,1,3:T(2,128)} async-done(((f32[2,1,128,1024]{2,0,1,3:T(2,128)}), f32[2,1,128,1024]{2,0,1,3:T(2,128)}, u32[]{:S(2)}, u32[]{:S(2)}) %all-to-all-start.2) | async-done | bytes 1048608 | tf_op jit(solution)/shard_map/all_to_all | solution.py:23
  56.6 3.6 %all-to-all-start = ((f32[2,1,136,1024]{2,0,1,3:T(2,128)}), f32[2,1,136,1024]{2,0,1,3:T(2,128)S(1)}, u32[]{:S(2)}, u32[]{:S(2)}) async-start(f32[2,1,136,1024]{2,0,1,3:T(2,128)} %copy.105), calls=%async_computation | async-start | bytes 4194304 | tf_op jit(solution)/shard_map/all_to_all | solution.py:21
  60.2 0.0 reduce-scatter.5.cloned.1.call-start
  60.2 0.0 copy-done.4
  60.2 1.6 convert_bitcast_fusion
  61.9 2.9 copy.109
  64.8 2.3 copy.114
  67.0 20.2 %all-to-all-done = f32[2,1,136,1024]{2,0,1,3:T(2,128)S(1)} async-done(((f32[2,1,136,1024]{2,0,1,3:T(2,128)}), f32[2,1,136,1024]{2,0,1,3:T(2,128)S(1)}, u32[]{:S(2)}, u32[]{:S(2)}) %all-to-all-start) | async-done | bytes 1114144 | tf_op jit(solution)/shard_map/all_to_all | solution.py:21
  87.3 0.2 copy.106
  87.4 0.0 copy-start
  87.4 0.1 multiply_reduce_fusion
  87.6 0.1 add_divide_fusion.1
  87.7 1.1 copy-done
  88.8 0.6 broadcast_in_dim.5
  89.4 1.2 stack_reshape.7
  90.6 0.6 broadcast_in_dim.4
  91.2 0.0 copy-start.3
  91.2 1.2 stack_reshape.6
  92.4 0.2 copy.107
  92.6 0.0 all-gather.2.cloned.1.call-done
  92.7 0.0 copy-done.3
  92.7 0.0 copy-start.1
  92.7 42.6 %fusion.50 = f32[2,8,128,128]{2,3,1,0:T(8,128)S(1)} fusion(f32[2,8,128,128]{2,3,1,0:T(8,128)S(1)} %bitcast.74, bf16[256,4096]{1,0:T(8,128)(2,1)} %all-gather.2.cloned.1.call-done, f32[4096,128]{1,0:T(8,128)} %bitcast.69, f32[2,8,4096]{2,0,1:T(2,128)S(1)} %copy.107), kind=kOutput, calls=%fused_computation.32 | convolution fusion | flops 6451101696 | bytes 5505024 | tf_op jit(solution)/shard_map/rk,pfkj->pfrj/dot_general | solution.py:38
  135.3 0.0 copy-start.6
  135.3 1.0 copy-done.6
  136.3 0.0 copy-done.1
  136.3 26.0 %fusion.35 = f32[128,4096]{1,0:T(8,128)} fusion(f32[4096,128]{1,0:T(8,128)S(1)} %bitcast.71, f32[2,8,4096]{2,0,1:T(2,128)S(1)} %copy.107, f32[2,8,128,128]{2,3,1,0:T(8,128)S(1)} %fusion.50), kind=kOutput, calls=%fused_computation.26 | convolution fusion | flops 6451363840 | bytes 5505024 | tf_op jit(solution)/shard_map/pfrj,pfkj->rk/dot_general | solution.py:41
  162.3 0.0 reduce-scatter.5.cloned.1.call-update
  162.4 0.0 reduce-scatter.3.cloned.1.call-start
  162.4 3.4 slice_convert_fusion
  165.8 2.9 copy.117
  168.7 0.0 copy-start.2
  168.7 29.0 %fusion.53 = f32[2,8,128,128]{2,3,1,0:T(8,128)S(1)} fusion(f32[2,8,136,128]{2,3,1,0:T(8,128)} %bitcast.68, bf16[256,4096]{1,0:T(8,128)(2,1)} %all-gather.2.cloned.1.call-done, f32[4096,128]{1,0:T(8,128)} %bitcast.70, f32[2,8,4096]{2,0,1:T(2,128)S(1)} %copy.107), kind=kOutput, calls=%fused_computation.33 | convolution fusion | flops 6451101696 | bytes 5505024 | tf_op jit(solution)/shard_map/rk,pfkj->pfrj/dot_general | solution.py:38
  197.7 0.0 copy-done.2
  197.7 25.8 %fusion.38 = f32[128,4096]{1,0:T(8,128)} fusion(f32[4096,128]{1,0:T(8,128)S(1)} %bitcast.72, f32[2,8,4096]{2,0,1:T(2,128)S(1)} %copy.107, f32[2,8,128,128]{2,3,1,0:T(8,128)S(1)} %fusion.53), kind=kOutput, calls=%fused_computation.27 | convolution fusion | flops 6451363840 | bytes 5505024 | tf_op jit(solution)/shard_map/pfrj,pfkj->rk/dot_general | solution.py:41
  223.5 0.0 reduce-scatter.3.cloned.1.call-update
  223.5 20.3 %fusion.26 = f32[4096,128]{1,0:T(8,128)} fusion(f32[128,4096]{0,1:T(8,128)} %copy.117, f32[2,8,4096]{2,0,1:T(2,128)S(1)} %copy.107, f32[2,8,128,128]{2,3,1,0:T(8,128)S(1)} %fusion.53), kind=kOutput, calls=%fused_computation.23 | convolution fusion | flops 6450839552 | bytes 5505024 | tf_op jit(solution)/shard_map/pfrk,pfrj->kj/dot_general | solution.py:46
  243.8 0.0 copy-start.7
  243.8 1.8 copy.119
  245.6 0.0 copy-done.7
  245.6 20.3 %fusion.41 = f32[4096,128]{1,0:T(8,128)S(1)} fusion(f32[4096,128]{1,0:T(8,128)} %fusion.26, f32[128,4096]{0,1:T(8,128)} %copy.119, f32[2,8,4096]{2,0,1:T(2,128)S(1)} %copy.107, f32[2,8,128,128]{2,3,1,0:T(8,128)S(1)} %copy-done.7), kind=kOutput, calls=%fused_computation.28 | convolution fusion | flops 6451888128 | bytes 7602176 | tf_op jit(solution)/shard_map/pfrk,pfrj->kj/dot_general | solution.py:46
  265.9 0.1 copy.121
  266.0 34.3 %all_to_all.69 = f32[8,8,64,128]{3,2,0,1:T(8,128)S(1)} all-to-all(f32[8,8,64,128]{3,2,0,1:T(8,128)S(1)} %copy.121), channel_id=1, replica_groups=mesh['freq'=8,'outp'=8,'inp'=2] {'outp'}, dimensions={1} | all-to-all | bytes 4194304 | tf_op jit(solution)/shard_map/all_to_all | solution.py:53
  300.4 0.1 reduce_sum.9
  300.5 11.5 %all_to_all.70 = f32[8,64,128]{2,1,0:T(8,128)S(1)} all-to-all(f32[8,64,128]{2,1,0:T(8,128)S(1)} %reduce_sum.9), channel_id=1, replica_groups=mesh['freq'=8,'outp'=8,'inp'=2] {'freq'}, dimensions={0} | all-to-all | bytes 524288 | tf_op jit(solution)/shard_map/all_to_all | solution.py:55
  312.0 0.2 copy.123
  312.1 0.8 copy.166
  312.9 0.0 reduce-scatter.5.cloned.1.call-done
  312.9 18.7 %reduce-scatter.3.cloned.1.call-done = f32[128,256]{1,0:T(8,128)} async-done(((f32[128,4096]{1,0:T(8,128)}), f32[128,256]{1,0:T(8,128)}) %reduce-scatter.3.cloned.1.call-update) | async-done | bytes 131088 | tf_op jit(solution)/shard_map/reduce_scatter | solution.py:43
  331.6 1.7 pad_maximum_fusion.1
  (2 shorter events, 0.0 us)
Async XLA Ops:
  7.2 85.5 %all-gather.2.cloned.1.call-start = ((), (), s32[]{:S(2)}) async-start(), calls=%async_computation.7 | async-start | bytes 2359296 | tf_op jit(solution)/shard_map/all_gather | solution.py:25
  10.2 4.7 %slice-start = ((f32[2,1,256,1024]{3,2,1,0:T(8,128)}), f32[2,1,128,1024]{3,2,1,0:T(8,128)S(1)}, s32[]{:S(2)}) async-start(f32[2,1,256,1024]{3,2,1,0:T(8,128)} %param.5), calls=%async_computation.10 | async-start | bytes 2097152 | tf_op jit(solution)/shard_map/slice | solution.py:23
  10.2 26.2 %all-to-all-start.1 = ((bf16[512,8,128]{0,2,1:T(8,128)(2,1)}), bf16[512,8,128]{0,2,1:T(8,128)(2,1)S(1)}, u32[]{:S(2)}, u32[]{:S(2)}) async-start(bf16[512,8,128]{0,2,1:T(8,128)(2,1)} %bitcast.4), calls=%async_computation.1 | async-start | bytes 2097152 | tf_op jit(solution)/shard_map/all_to_all | solution.py:24
  14.9 26.4 %copy-start.5 = (pred[136]{0:T(512)(128)(4,1)S(1)}, pred[136]{0:T(512)(128)(4,1)}, u32[]{:S(2)}) copy-start(pred[136]{0:T(512)(128)(4,1)} %constant.1.clone.1) | copy-start | bytes 412
  36.4 20.2 %all-to-all-start.2 = ((f32[2,1,128,1024]{2,0,1,3:T(2,128)}), f32[2,1,128,1024]{2,0,1,3:T(2,128)}, u32[]{:S(2)}, u32[]{:S(2)}) async-start(f32[2,1,128,1024]{2,0,1,3:T(2,128)} %copy.143), calls=%async_computation.3 | async-start | bytes 2097152 | tf_op jit(solution)/shard_map/all_to_all | solution.py:23
  45.0 15.3 %copy-start.4 = (f32[512]{0:T(512)S(1)}, f32[512]{0:T(512)}, u32[]{:S(2)}) copy-start(f32[512]{0:T(512)} %param.8) | copy-start | bytes 6148
  56.6 30.7 %all-to-all-start = ((f32[2,1,136,1024]{2,0,1,3:T(2,128)}), f32[2,1,136,1024]{2,0,1,3:T(2,128)S(1)}, u32[]{:S(2)}, u32[]{:S(2)}) async-start(f32[2,1,136,1024]{2,0,1,3:T(2,128)} %copy.105), calls=%async_computation | async-start | bytes 4194304 | tf_op jit(solution)/shard_map/all_to_all | solution.py:21
  60.2 252.7 %reduce-scatter.5.cloned.1.call-start = ((), (), s32[]{:S(2)}) async-start(), calls=%async_computation.9 | async-start | bytes 2228224 | tf_op jit(solution)/shard_map/reduce_scatter | solution.py:43
  87.4 1.3 copy-start
  91.2 1.5 copy-start.3
  92.7 43.7 %copy-start.1 = (f32[8,512,128]{2,1,0:T(8,128)S(1)}, f32[8,512,128]{2,1,0:T(8,128)}, u32[]{:S(2)}) copy-start(f32[8,512,128]{2,1,0:T(8,128)} %copy.109) | copy-start | bytes 6291460
  135.3 1.1 copy-start.6
  162.4 169.2 %reduce-scatter.3.cloned.1.call-start = ((), (), s32[]{:S(2)}) async-start(), calls=%async_computation.8 | async-start | bytes 2228224 | tf_op jit(solution)/shard_map/reduce_scatter | solution.py:43
  168.7 29.0 %copy-start.2 = (f32[8,512,128]{2,1,0:T(8,128)S(1)}, f32[8,512,128]{2,1,0:T(8,128)}, u32[]{:S(2)}) copy-start(f32[8,512,128]{2,1,0:T(8,128)} %copy.109) | copy-start | bytes 6291460
  243.8 1.8 copy-start.7
Sparse Core Ops, SparseCore 0:
  9.7 31.0 all-gather.1
  162.5 72.5 reduce-scatter.4
  239.0 92.5 reduce-scatter.2

commit v4 on v2

--- a/solution.py
+++ b/solution.py
@@ -36,16 +36,15 @@
     misfit = fitted - observed
     grad_left = jnp.einsum("pfrj,pfkj->rk", misfit, scaled_right, precision=highest,
                            preferred_element_type=jnp.float32)
+    grad_left = lax.psum_scatter(grad_left * grad_scale, ("freq", "inp"), scatter_dimension=1, tiled=True)
     scaled_left = resp[:, :, None, :] * left_wide[None, None]
     grad_right = jnp.einsum("pfrk,pfrj->kj", scaled_left, misfit, precision=highest,
                             preferred_element_type=jnp.float32)
-    grad_left = lax.psum_scatter(grad_left * grad_scale, ("freq", "inp"), scatter_dimension=1, tiled=True)
     k_rows, j_cols = grad_right.shape
     block = k_rows // (n_freq * n_outp)
     grad_right = (grad_right * grad_scale).reshape(n_freq, n_outp, block, j_cols)
-    grad_right = grad_right.transpose(1, 0, 2, 3).reshape(n_outp * n_freq * block, j_cols)
-    grad_right = lax.psum_scatter(grad_right, "outp", scatter_dimension=0, tiled=True)
-    grad_right = grad_right.reshape(n_freq, block, j_cols)
+    grad_right = lax.all_to_all(grad_right, "outp", 1, 1, tiled=True)
+    grad_right = jnp.sum(grad_right, axis=1)
     grad_right = lax.all_to_all(grad_right, "freq", 0, 2, tiled=True)
     grad_right = grad_right.reshape(block, n_freq * j_cols)
     return (grad_left, grad_right)

time: 305 us -> 271 us (0.89)
  waiting for transfers between devices: 135 us -> 69.1 us
  blocking collectives: 12.6 us -> 46.6 us
    reduce_scatter x1, waiting for transfers between devices: 72.8 us -> 20.8 us  [shards(): lax.psum_scatter(grad_left * grad_scale, ('freq', 'inp'), scatter_dimensi...]
    all_to_all x0 -> x1, blocking collectives: none -> 34.9 us  [shards(): grad_right = lax.all_to_all(grad_right, 'outp', 1, 1, tiled=True)]
    reduce_scatter x1 -> x0, waiting for transfers between devices: 13.6 us -> none  [shards(): lax.psum_scatter(grad_right, 'outp', scatter_dimension=0, tiled=True)]
  transfers between devices with their start and end apart: 5 -> 4, of which waited for: 4 -> 3; matrix products, arithmetic and copies ran while one was open for 19% -> 20% of each run, Pallas kernels for 0% -> 0%
where the time goes in v4:
time: 271 us; the launch traced here: 266 us
  matrix products  99 us (37%)
  waiting for transfers between devices  69.1 us (25%)
  blocking collectives  46.6 us (17%)
  local copies, waits for them, and re-layouts  24 us (9%)
  between operations  15.3 us (6%)
  starting transfers between devices  8.31 us (3%)
  other arithmetic  3.25 us (1%)
    dot_general x1, matrix products, shards(): jnp.einsum('pfrj,pfkj->rk', misfit, scaled_right, precision=highest, pref...  37.3 us
    all_to_all x1, blocking collectives, shards(): grad_right = lax.all_to_all(grad_right, 'outp', 1, 1, tiled=True)  34.9 us
    all_to_all x1, waiting for transfers between devices, shards(): tagged = lax.all_to_all(tagged, 'freq', 3, 1, tiled=True)  32.5 us
    dot_general x1, matrix products, shards(): jnp.einsum('pfrk,pfrj->kj', scaled_left, misfit, precision=highest, prefe...  32 us
    dot_general x1, matrix products, shards(): jnp.einsum('rk,pfkj->pfrj', left_wide, scaled_right, precision=highest, p...  29.7 us
    reduce_scatter x1, waiting for transfers between devices, shards(): lax.psum_scatter(grad_left * grad_scale, ('freq', 'inp'), scatter_dimensi...  20.8 us
    all_to_all x1, waiting for transfers between devices, shards(): right_cols = lax.all_to_all(right_factor, 'freq', 1, 0, tiled=True)  15.2 us
    all_to_all x1, blocking collectives, shards(): grad_right = lax.all_to_all(grad_right, 'freq', 0, 2, tiled=True)  11.7 us
  transfers between devices with their start and end apart: 4, of which 3 were waited for; matrix products, arithmetic and copies ran while one was open for 20% of the time, Pallas kernels for 0%

profile of v4, /device:TPU:0, one launch (start us, length us, event | category | flops | bytes accessed | tf_op | source)
XLA Modules:
  0.0 265.6 jit_solution(17876081682636682394)
XLA Ops:
  7.2 0.0 all-gather.2.cloned.1.call-start
  7.2 0.7 all-gather.2.cloned.1.call-update
  7.9 2.3 copy.56
  10.2 4.6 %all-to-all-start.1 = ((bf16[512,8,128]{0,2,1:T(8,128)(2,1)}), bf16[512,8,128]{0,2,1:T(8,128)(2,1)S(1)}, u32[]{:S(2)}, u32[]{:S(2)}) async-start(bf16[512,8,128]{0,2,1:T(8,128)(2,1)} %bitcast.4), calls=%async_computation.1 | async-start | bytes 2097152 | tf_op jit(solution)/shard_map/all_to_all | solution.py:23
  15.4 2.9 %copy.53 = f32[2,1,256,1024]{2,0,1,3:T(2,128)S(1)} copy(f32[2,1,256,1024]{3,2,1,0:T(8,128)} %param.5) | data formatting | bytes 4194304 | tf_op args[0]
  18.3 2.6 concatenate.3
  20.9 0.0 copy-start.4
  20.9 15.2 %all-to-all-done.1 = bf16[512,8,128]{0,2,1:T(8,128)(2,1)S(1)} async-done(((bf16[512,8,128]{0,2,1:T(8,128)(2,1)}), bf16[512,8,128]{0,2,1:T(8,128)(2,1)S(1)}, u32[]{:S(2)}, u32[]{:S(2)}) %all-to-all-start.1) | async-done | bytes 1048608 | tf_op jit(solution)/shard_map/all_to_all | solution.py:23
  36.1 0.0 copy-start
  36.1 1.0 copy-done
  37.1 3.6 %all-to-all-start = ((f32[2,1,264,1024]{2,0,1,3:T(2,128)}), f32[2,1,264,1024]{2,0,1,3:T(2,128)S(1)}, u32[]{:S(2)}, u32[]{:S(2)}) async-start(f32[2,1,264,1024]{2,0,1,3:T(2,128)} %concatenate.3), calls=%async_computation | async-start | bytes 6291456 | tf_op jit(solution)/shard_map/all_to_all | solution.py:20
  40.7 0.0 reduce-scatter.2.cloned.1.call-start
  40.8 0.0 copy-done.4
  40.8 2.9 %convert_bitcast_fusion = f32[8,512,128]{1,2,0:T(8,128)} fusion(bf16[512,8,128]{0,2,1:T(8,128)(2,1)} %copy-done), kind=kLoop, calls=%fused_computation.14 | loop fusion | flops 524288 | bytes 3145728 | tf_op jit(solution)/shard_map/convert_element_type | solution.py:28
  43.7 2.9 %copy.57 = f32[8,512,128]{2,1,0:T(8,128)} copy(f32[8,512,128]{1,2,0:T(8,128)} %convert_bitcast_fusion) | data formatting | bytes 4194304 | tf_op jit(solution)/shard_map/convert_element_type | solution.py:28
  46.6 32.5 %all-to-all-done = f32[2,1,264,1024]{2,0,1,3:T(2,128)S(1)} async-done(((f32[2,1,264,1024]{2,0,1,3:T(2,128)}), f32[2,1,264,1024]{2,0,1,3:T(2,128)S(1)}, u32[]{:S(2)}, u32[]{:S(2)}) %all-to-all-start) | async-done | bytes 2162720 | tf_op jit(solution)/shard_map/all_to_all | solution.py:20
  79.1 0.2 copy.54
  79.3 0.0 copy-start.1
  79.3 0.1 multiply_reduce_fusion
  79.4 0.1 add_divide_fusion.1
  79.5 1.4 copy-done.1
  80.9 0.6 broadcast_in_dim.4
  81.5 1.2 stack_reshape.6
  82.7 0.6 broadcast_in_dim.5
  83.3 1.2 stack_reshape.7
  84.5 0.2 copy.55
  84.8 0.0 all-gather.2.cloned.1.call-done
  84.8 0.0 copy-start.3
  84.8 29.7 %slice_subtract_fusion = f32[2,8,256,128]{2,3,1,0:T(8,128)S(1)} fusion(f32[2,8,264,128]{2,3,1,0:T(8,128)} %bitcast.42, bf16[256,4096]{1,0:T(8,128)(2,1)} %all-gather.2.cloned.1.call-done, f32[4096,128]{1,0:T(8,128)} %bitcast.43, f32[2,8,4096]{2,0,1:T(2,128)S(1)} %copy.55), kind=kOutput, calls=%fused_computation.12 | convolution fusion | flops 12893814784 | bytes 8650752 | tf_op jit(solution)/shard_map/rk,pfkj->pfrj/dot_general | solution.py:34
  114.5 0.0 copy-start.5
  114.5 1.3 copy-done.5
  115.8 0.0 copy-done.3
  115.8 37.3 %fusion.8 = f32[256,4096]{1,0:T(8,128)} fusion(f32[4096,128]{1,0:T(8,128)S(1)} %bitcast.44, f32[2,8,4096]{2,0,1:T(2,128)S(1)} %copy.55, f32[2,8,256,128]{2,3,1,0:T(8,128)S(1)} %slice_subtract_fusion), kind=kOutput, calls=%fused_computation.9 | convolution fusion | flops 12894339072 | bytes 8650752 | tf_op jit(solution)/shard_map/pfrj,pfkj->rk/dot_general | solution.py:37
  153.1 0.0 copy-start.2
  153.1 0.0 reduce-scatter.2.cloned.1.call-update
  153.2 1.6 copy-done.2
  154.7 3.0 %copy.61 = f32[256,4096]{0,1:T(8,128)} copy(bf16[256,4096]{1,0:T(8,128)(2,1)S(1)} %copy-done.2) | data formatting | bytes 6291456 | tf_op jit(solution)/shard_map/convert_element_type | solution.py:27
  157.7 32.0 %fusion.12 = f32[4096,128]{1,0:T(8,128)S(1)} fusion(f32[256,4096]{0,1:T(8,128)} %copy.61, f32[2,8,4096]{2,0,1:T(2,128)S(1)} %copy.55, f32[2,8,256,128]{2,3,1,0:T(8,128)} %copy-done.5), kind=kOutput, calls=%fused_computation.11 | convolution fusion | flops 12902203392 | bytes 8650752 | tf_op jit(solution)/shard_map/pfrk,pfrj->kj/dot_general | solution.py:41
  189.7 0.1 copy.63
  189.8 34.9 %all_to_all.51 = f32[8,8,64,128]{3,2,0,1:T(8,128)S(1)} all-to-all(f32[8,8,64,128]{3,2,0,1:T(8,128)S(1)} %copy.63), channel_id=1, replica_groups=mesh['freq'=8,'outp'=8,'inp'=2] {'outp'}, dimensions={1} | all-to-all | bytes 4194304 | tf_op jit(solution)/shard_map/all_to_all | solution.py:46
  224.7 0.1 reduce_sum.9
  224.9 11.7 %all_to_all.52 = f32[8,64,128]{2,1,0:T(8,128)S(1)} all-to-all(f32[8,64,128]{2,1,0:T(8,128)S(1)} %reduce_sum.9), channel_id=1, replica_groups=mesh['freq'=8,'outp'=8,'inp'=2] {'freq'}, dimensions={0} | all-to-all | bytes 524288 | tf_op jit(solution)/shard_map/all_to_all | solution.py:48
  236.6 0.2 copy.65
  236.8 0.8 copy.86
  237.5 20.8 %reduce-scatter.2.cloned.1.call-done = f32[256,256]{1,0:T(8,128)} async-done(((f32[256,4096]{1,0:T(8,128)}), f32[256,256]{1,0:T(8,128)}) %reduce-scatter.2.cloned.1.call-update) | async-done | bytes 262160 | tf_op jit(solution)/shard_map/reduce_scatter | solution.py:39
  (2 shorter events, 0.0 us)
Async XLA Ops:
  7.2 77.6 %all-gather.2.cloned.1.call-start = ((), (), s32[]{:S(2)}) async-start(), calls=%async_computation.5 | async-start | bytes 2359296 | tf_op jit(solution)/shard_map/all_gather | solution.py:24
  10.2 25.9 %all-to-all-start.1 = ((bf16[512,8,128]{0,2,1:T(8,128)(2,1)}), bf16[512,8,128]{0,2,1:T(8,128)(2,1)S(1)}, u32[]{:S(2)}, u32[]{:S(2)}) async-start(bf16[512,8,128]{0,2,1:T(8,128)(2,1)} %bitcast.4), calls=%async_computation.1 | async-start | bytes 2097152 | tf_op jit(solution)/shard_map/all_to_all | solution.py:23
  20.9 19.9 %copy-start.4 = (f32[512]{0:T(512)S(1)}, f32[512]{0:T(512)}, u32[]{:S(2)}) copy-start(f32[512]{0:T(512)} %param.8) | copy-start | bytes 6148
  36.1 1.0 copy-start
  37.1 42.0 %all-to-all-start = ((f32[2,1,264,1024]{2,0,1,3:T(2,128)}), f32[2,1,264,1024]{2,0,1,3:T(2,128)S(1)}, u32[]{:S(2)}, u32[]{:S(2)}) async-start(f32[2,1,264,1024]{2,0,1,3:T(2,128)} %concatenate.3), calls=%async_computation | async-start | bytes 6291456 | tf_op jit(solution)/shard_map/all_to_all | solution.py:20
  40.7 217.6 %reduce-scatter.2.cloned.1.call-start = ((), (), s32[]{:S(2)}) async-start(), calls=%async_computation.6 | async-start | bytes 4456448 | tf_op jit(solution)/shard_map/reduce_scatter | solution.py:39
  79.3 1.7 copy-start.1
  84.8 31.0 %copy-start.3 = (f32[8,512,128]{2,1,0:T(8,128)S(1)}, f32[8,512,128]{2,1,0:T(8,128)}, u32[]{:S(2)}) copy-start(f32[8,512,128]{2,1,0:T(8,128)} %copy.57) | copy-start | bytes 6291460
  114.5 1.4 copy-start.5
  153.1 1.6 copy-start.2
Sparse Core Ops, SparseCore 0:
  9.7 30.9 all-gather.1
  153.3 104.9 reduce-scatter.1

commit v5 on v4

--- a/solution.py
+++ b/solution.py
@@ -15,12 +15,15 @@
     n_freq = lax.axis_size("freq")
     n_outp = lax.axis_size("outp")
     two, _, out_rows, in_cols = measured.shape
+    k_block, _ = right_factor.shape
+    chunks = right_factor.reshape(k_block, n_freq, in_cols // n_freq).transpose(1, 0, 2)
+    chunks = lax.all_to_all(chunks, "freq", 0, 0, tiled=True)
+    right_cols = chunks.reshape(n_freq * k_block, in_cols // n_freq)
     tagged = jnp.concatenate(
         [measured, jnp.broadcast_to(sample_freqs[0], (two, 1, 8, in_cols))], axis=2)
     tagged = lax.all_to_all(tagged, "freq", 3, 1, tiled=True)
     observed = tagged[:, :, :out_rows, :]
     omegas = tagged[0, :, out_rows, 0]
-    right_cols = lax.all_to_all(right_factor, "freq", 1, 0, tiled=True)
     left_whole = lax.all_gather(left_factor, "freq", axis=1, tiled=True)
     total_samples = omegas.shape[0]
     grad_scale = float(RANKS) ** 0.25 / math.sqrt(float(total_samples * PORTS))

time: 271 us -> 271 us (level)
  waiting for transfers between devices: 69.1 us -> 72.3 us
  other arithmetic: 3.25 us -> 0.38 us
    all_to_all x1, waiting for transfers between devices: 32.5 us -> 35.7 us  [shards(): tagged = lax.all_to_all(tagged, 'freq', 3, 1, tiled=True)]
    convert_element_type x1 -> x0, other arithmetic: 2.87 us -> none  [shards(): right_wide = right_cols.astype(jnp.float32)]
  transfers between devices with their start and end apart: 4 -> 4, of which waited for: 3 -> 3; matrix products, arithmetic and copies ran while one was open for 20% -> 19% of each run, Pallas kernels for 0% -> 0%
where the time goes in v5:
time: 271 us; the launch traced here: 266 us
  matrix products  99 us (37%)
  waiting for transfers between devices  72.3 us (27%)
  blocking collectives  46.6 us (17%)
  local copies, waits for them, and re-layouts  23.7 us (9%)
  between operations  15.3 us (6%)
  starting transfers between devices  8.31 us (3%)
    dot_general x1, matrix products, shards(): jnp.einsum('pfrj,pfkj->rk', misfit, scaled_right, precision=highest, pref...  37.3 us
    all_to_all x1, waiting for transfers between devices, shards(): tagged = lax.all_to_all(tagged, 'freq', 3, 1, tiled=True)  35.7 us
    all_to_all x1, blocking collectives, shards(): grad_right = lax.all_to_all(grad_right, 'outp', 1, 1, tiled=True)  34.9 us
    dot_general x1, matrix products, shards(): jnp.einsum('pfrk,pfrj->kj', scaled_left, misfit, precision=highest, prefe...  32 us
    dot_general x1, matrix products, shards(): jnp.einsum('rk,pfkj->pfrj', left_wide, scaled_right, precision=highest, p...  29.7 us
    reduce_scatter x1, waiting for transfers between devices, shards(): lax.psum_scatter(grad_left * grad_scale, ('freq', 'inp'), scatter_dimensi...  20.8 us
    all_to_all x1, waiting for transfers between devices, shards(): chunks = lax.all_to_all(chunks, 'freq', 0, 0, tiled=True)  15.2 us
    all_to_all x1, blocking collectives, shards(): grad_right = lax.all_to_all(grad_right, 'freq', 0, 2, tiled=True)  11.7 us
  transfers between devices with their start and end apart: 4, of which 3 were waited for; matrix products, arithmetic and copies ran while one was open for 19% of the time, Pallas kernels for 0%

profile of v5, /device:TPU:0, one launch (start us, length us, event | category | flops | bytes accessed | tf_op | source)
XLA Modules:
  0.0 265.6 jit_solution(9288781599065048683)
XLA Ops:
  7.2 0.0 all-gather.2.cloned.1.call-start
  7.2 0.7 all-gather.2.cloned.1.call-update
  7.9 2.3 copy.56
  10.2 4.6 %all-to-all-start.1 = ((bf16[8,512,128]{1,2,0:T(8,128)(2,1)}), bf16[8,512,128]{1,2,0:T(8,128)(2,1)S(1)}, u32[]{:S(2)}, u32[]{:S(2)}) async-start(bf16[8,512,128]{1,2,0:T(8,128)(2,1)} %bitcast.5), calls=%async_computation.1 | async-start | bytes 2097152 | tf_op jit(solution)/shard_map/all_to_all | solution.py:20
  15.4 2.9 %copy.53 = f32[2,1,256,1024]{2,0,1,3:T(2,128)S(1)} copy(f32[2,1,256,1024]{3,2,1,0:T(8,128)} %param.5) | data formatting | bytes 4194304 | tf_op args[0]
  18.3 2.6 concatenate.3
  20.9 0.0 copy-start.4
  20.9 15.2 %all-to-all-done.1 = bf16[8,512,128]{1,2,0:T(8,128)(2,1)S(1)} async-done(((bf16[8,512,128]{1,2,0:T(8,128)(2,1)}), bf16[8,512,128]{1,2,0:T(8,128)(2,1)S(1)}, u32[]{:S(2)}, u32[]{:S(2)}) %all-to-all-start.1) | async-done | bytes 1048608 | tf_op jit(solution)/shard_map/all_to_all | solution.py:20
  36.1 0.0 copy-start
  36.1 1.0 copy-done
  37.1 3.6 %all-to-all-start = ((f32[2,1,264,1024]{2,0,1,3:T(2,128)}), f32[2,1,264,1024]{2,0,1,3:T(2,128)S(1)}, u32[]{:S(2)}, u32[]{:S(2)}) async-start(f32[2,1,264,1024]{2,0,1,3:T(2,128)} %concatenate.3), calls=%async_computation | async-start | bytes 6291456 | tf_op jit(solution)/shard_map/all_to_all | solution.py:24
  40.7 0.0 reduce-scatter.2.cloned.1.call-start
  40.8 0.0 copy-done.4
  40.8 2.6 copy.57
  43.4 35.7 %all-to-all-done = f32[2,1,264,1024]{2,0,1,3:T(2,128)S(1)} async-done(((f32[2,1,264,1024]{2,0,1,3:T(2,128)}), f32[2,1,264,1024]{2,0,1,3:T(2,128)S(1)}, u32[]{:S(2)}, u32[]{:S(2)}) %all-to-all-start) | async-done | bytes 2162720 | tf_op jit(solution)/shard_map/all_to_all | solution.py:24
  79.1 0.2 copy.54
  79.3 0.0 copy-start.1
  79.3 0.1 multiply_reduce_fusion
  79.4 0.1 add_divide_fusion.1
  79.5 1.4 copy-done.1
  80.9 0.6 broadcast_in_dim.4
  81.5 1.2 stack_reshape.6
  82.7 0.6 broadcast_in_dim.5
  83.3 1.2 stack_reshape.7
  84.5 0.2 copy.55
  84.8 0.0 all-gather.2.cloned.1.call-done
  84.8 0.0 copy-start.3
  84.8 29.7 %slice_subtract_fusion = f32[2,8,256,128]{2,3,1,0:T(8,128)S(1)} fusion(f32[2,8,264,128]{2,3,1,0:T(8,128)} %bitcast.42, bf16[256,4096]{1,0:T(8,128)(2,1)} %all-gather.2.cloned.1.call-done, f32[4096,128]{1,0:T(8,128)} %bitcast.43, f32[2,8,4096]{2,0,1:T(2,128)S(1)} %copy.55), kind=kOutput, calls=%fused_computation.12 | convolution fusion | flops 12893814784 | bytes 8650752 | tf_op jit(solution)/shard_map/rk,pfkj->pfrj/dot_general | solution.py:37
  114.5 0.0 copy-start.5
  114.5 1.3 copy-done.5
  115.8 0.0 copy-done.3
  115.8 37.3 %fusion.8 = f32[256,4096]{1,0:T(8,128)} fusion(f32[4096,128]{1,0:T(8,128)S(1)} %bitcast.44, f32[2,8,4096]{2,0,1:T(2,128)S(1)} %copy.55, f32[2,8,256,128]{2,3,1,0:T(8,128)S(1)} %slice_subtract_fusion), kind=kOutput, calls=%fused_computation.9 | convolution fusion | flops 12894339072 | bytes 8650752 | tf_op jit(solution)/shard_map/pfrj,pfkj->rk/dot_general | solution.py:40
  153.1 0.0 copy-start.2
  153.1 0.0 reduce-scatter.2.cloned.1.call-update
  153.2 1.6 copy-done.2
  154.7 3.0 %copy.61 = f32[256,4096]{0,1:T(8,128)} copy(bf16[256,4096]{1,0:T(8,128)(2,1)S(1)} %copy-done.2) | data formatting | bytes 6291456 | tf_op jit(solution)/shard_map/convert_element_type | solution.py:30
  157.7 32.0 %fusion.12 = f32[4096,128]{1,0:T(8,128)S(1)} fusion(f32[256,4096]{0,1:T(8,128)} %copy.61, f32[2,8,4096]{2,0,1:T(2,128)S(1)} %copy.55, f32[2,8,256,128]{2,3,1,0:T(8,128)} %copy-done.5), kind=kOutput, calls=%fused_computation.11 | convolution fusion | flops 12902203392 | bytes 8650752 | tf_op jit(solution)/shard_map/pfrk,pfrj->kj/dot_general | solution.py:44
  189.7 0.1 copy.63
  189.8 34.9 %all_to_all.43 = f32[8,8,64,128]{3,2,0,1:T(8,128)S(1)} all-to-all(f32[8,8,64,128]{3,2,0,1:T(8,128)S(1)} %copy.63), channel_id=1, replica_groups=mesh['freq'=8,'outp'=8,'inp'=2] {'outp'}, dimensions={1} | all-to-all | bytes 4194304 | tf_op jit(solution)/shard_map/all_to_all | solution.py:49
  224.7 0.1 reduce_sum.9
  224.9 11.7 %all_to_all.44 = f32[8,64,128]{2,1,0:T(8,128)S(1)} all-to-all(f32[8,64,128]{2,1,0:T(8,128)S(1)} %reduce_sum.9), channel_id=1, replica_groups=mesh['freq'=8,'outp'=8,'inp'=2] {'freq'}, dimensions={0} | all-to-all | bytes 524288 | tf_op jit(solution)/shard_map/all_to_all | solution.py:51
  236.6 0.2 copy.65
  236.8 0.8 copy.86
  237.5 20.8 %reduce-scatter.2.cloned.1.call-done = f32[256,256]{1,0:T(8,128)} async-done(((f32[256,4096]{1,0:T(8,128)}), f32[256,256]{1,0:T(8,128)}) %reduce-scatter.2.cloned.1.call-update) | async-done | bytes 262160 | tf_op jit(solution)/shard_map/reduce_scatter | solution.py:42
  (2 shorter events, 0.0 us)
Async XLA Ops:
  7.2 77.6 %all-gather.2.cloned.1.call-start = ((), (), s32[]{:S(2)}) async-start(), calls=%async_computation.5 | async-start | bytes 2359296 | tf_op jit(solution)/shard_map/all_gather | solution.py:27
  10.2 25.9 %all-to-all-start.1 = ((bf16[8,512,128]{1,2,0:T(8,128)(2,1)}), bf16[8,512,128]{1,2,0:T(8,128)(2,1)S(1)}, u32[]{:S(2)}, u32[]{:S(2)}) async-start(bf16[8,512,128]{1,2,0:T(8,128)(2,1)} %bitcast.5), calls=%async_computation.1 | async-start | bytes 2097152 | tf_op jit(solution)/shard_map/all_to_all | solution.py:20
  20.9 19.9 %copy-start.4 = (f32[512]{0:T(512)S(1)}, f32[512]{0:T(512)}, u32[]{:S(2)}) copy-start(f32[512]{0:T(512)} %param.8) | copy-start | bytes 6148
  36.1 1.0 copy-start
  37.1 42.0 %all-to-all-start = ((f32[2,1,264,1024]{2,0,1,3:T(2,128)}), f32[2,1,264,1024]{2,0,1,3:T(2,128)S(1)}, u32[]{:S(2)}, u32[]{:S(2)}) async-start(f32[2,1,264,1024]{2,0,1,3:T(2,128)} %concatenate.3), calls=%async_computation | async-start | bytes 6291456 | tf_op jit(solution)/shard_map/all_to_all | solution.py:24
  40.7 217.6 %reduce-scatter.2.cloned.1.call-start = ((), (), s32[]{:S(2)}) async-start(), calls=%async_computation.6 | async-start | bytes 4456448 | tf_op jit(solution)/shard_map/reduce_scatter | solution.py:42
  79.3 1.7 copy-start.1
  84.8 31.0 %copy-start.3 = (f32[8,512,128]{2,1,0:T(8,128)S(1)}, f32[8,512,128]{2,1,0:T(8,128)}, u32[]{:S(2)}) copy-start(f32[8,512,128]{2,1,0:T(8,128)} %copy.57) | copy-start | bytes 6291460
  114.5 1.4 copy-start.5
  153.1 1.6 copy-start.2
Sparse Core Ops, SparseCore 0:
  9.7 30.9 all-gather.1
  153.3 104.9 reduce-scatter.1
